TPU v7x, 512 devices: a whole 4x4x16 slice. The times are simulated.
512 devices in a mesh: ctx: 16 (over z), ep: 32 (over y, x, core).
Axes of the slice: x: 4, y: 4, z: 16, core: 2. Of those that a mesh axis runs over, the one named last changes fastest.
Arguments:
- query_act: bfloat16 [2048, 8192], P('ctx', 'ep'), may hold values from -6 to 6
- key_act: bfloat16 [2048, 8192], P('ctx', 'ep'), may hold values from -6 to 6
- value_act: bfloat16 [2048, 8192], P('ctx', 'ep'), may hold values from -6 to 6
- state_init: float32 [64, 128, 128], P('ep'), may hold values from -128 to 128
- head_gain: float32 [8192], P('ep'), may hold values from 0.25 to 1.75
- out_weight: bfloat16 [8192, 3072], P('ctx', 'ep'), may hold values from -0.0625 to 0.0625
- stream_in: bfloat16 [2048, 3072], P('ctx', 'ep'), may hold values from -150 to 150
- model_gain: float32 [3072], replicated, may hold values from 0.25 to 1.75
- expert_ids: int32 [2048, 2], P('ctx'), may hold values from 0 to 15, as said below
- expert_slots: int32 [2048, 2], P('ctx'), may hold values from 0 to 19, as said below
- route_gates: float32 [2048, 2], P('ctx'), may hold values from 0.2 to 1
- gate_weight: bfloat16 [32, 3072, 3072], P('ep', 'ctx'), may hold values from -0.109375 to 0.109375
- up_weight: bfloat16 [32, 3072, 3072], P('ep', 'ctx'), may hold values from -0.109375 to 0.109375
- down_weight: bfloat16 [32, 3072, 3072], P('ep', 'ctx'), may hold values from -0.078125 to 0.078125
- out_grad: bfloat16 [2048, 3072], P('ctx', 'ep'), may hold values from -6 to 6
Outputs:
- layer_out: bfloat16 [2048, 3072], P('ctx', 'ep')
- grad_query: bfloat16 [2048, 8192], P('ctx', 'ep')
- grad_key: bfloat16 [2048, 8192], P('ctx', 'ep')
- grad_value: bfloat16 [2048, 8192], P('ctx', 'ep')
- grad_state: float32 [64, 128, 128], P('ep')
- grad_stream: bfloat16 [2048, 3072], P('ctx', 'ep')
Inputs may be any that keep to these rules, and one draw needn't show every extreme that they name: `expert_ids`: within each block of 128 tokens a token's two experts differ; the tokens naming expert e hold the slots 0 to n - 1 of e once each, n being their number; no expert is named by more than 20 tokens of a block, and in every block some expert by exactly 20. `expert_slots`: see expert_ids.
All inputs are finite; a program needn't handle non-finite values.
Results may differ from a plain program's by a relative error of at most 0.02.
Values may be sent and summed in bfloat16 or wider, within the bound.
No kernel may reach another device: no remote copies, remote signals or barrier semaphores. Data moves between devices by JAX's collectives and lax.ppermute only.
A program may use at most 64 MiB of HBM per device.

v0:
```python
import jax
import jax.numpy as jnp
from jax import lax
from jax.sharding import PartitionSpec as P


def carried_in(value, axis, join, neutral, backward):
    count = lax.axis_size(axis)
    place = lax.axis_index(axis)
    ahead = count - 1 - place if backward else place
    gathered = lax.all_gather(value.astype(jnp.bfloat16), axis)
    state = jnp.zeros_like(value) + jnp.asarray(neutral, value.dtype)

    def one(turn, state):
        source = count - 1 - turn if backward else turn
        return join(state, lax.dynamic_index_in_dim(gathered, source, 0, False).astype(value.dtype))

    return lax.fori_loop(0, ahead, one, state)


def head_normalize(attended, gain):
    factor = lax.rsqrt(jnp.mean(attended * attended, -1, keepdims=True) + 1e-06)
    return attended * factor * gain


def add_states(earlier, later_one):
    return earlier + later_one


def contract_last(left, right):
    return lax.dot_general(
        left, right, (((1,), (1,)), ((), ())), preferred_element_type=jnp.float32
    )


def local(
    query_act,
    key_act,
    value_act,
    state_init,
    head_gain,
    out_weight,
    stream_in,
    model_gain,
    expert_ids,
    expert_slots,
    route_gates,
    gate_weight,
    up_weight,
    down_weight,
    out_grad,
):
    f32 = jnp.float32
    high = lax.Precision.HIGHEST
    ep_count = lax.axis_size("ep")
    expert_count = ep_count // 2
    my_ep = lax.axis_index("ep")
    tokens_here = query_act.shape[0]
    head_count = state_init.shape[0]
    head_size = state_init.shape[1]
    model_width = model_gain.shape[0]
    columns = stream_in.shape[1]
    capacity = 5 * tokens_here // (2 * expert_count)
    query3 = query_act.reshape(tokens_here, head_count, head_size)
    key3 = key_act.reshape(tokens_here, head_count, head_size)
    value3 = value_act.reshape(tokens_here, head_count, head_size)
    kv_own = jnp.einsum("thd,the->hde", key3, value3, preferred_element_type=f32)
    zero_state = jnp.zeros_like(kv_own)
    before = carried_in(kv_own, "ctx", add_states, zero_state, False)
    prefix = state_init + before
    causal = jnp.arange(tokens_here)[:, None] >= jnp.arange(tokens_here)[None, :]
    scores = jnp.einsum("thd,shd->hts", query3, key3, preferred_element_type=f32)
    scores_bf = jnp.where(causal[None], scores, 0.0).astype(jnp.bfloat16)
    inside = jnp.einsum("hts,she->the", scores_bf, value3, preferred_element_type=f32)
    from_state = jnp.einsum("thd,hde->the", query3.astype(f32), prefix, precision=high)
    attended = from_state + inside
    gain_heads = head_gain.reshape(head_count, head_size)
    normed_heads = (
        head_normalize(attended, gain_heads)
        .astype(jnp.bfloat16)
        .reshape(tokens_here, head_count * head_size)
    )
    w_cols = lax.all_gather(out_weight, "ctx", axis=0, tiled=True)
    attn_proj = jnp.dot(
        lax.all_gather(normed_heads, "ep", axis=1, tiled=True), w_cols, preferred_element_type=f32
    )
    stream = (stream_in.astype(f32) + attn_proj).astype(jnp.bfloat16)
    stream_f = stream.astype(f32)
    gain_cols = lax.dynamic_slice_in_dim(model_gain, my_ep * columns, columns, 0)
    dest_expert = jnp.arange(ep_count) % expert_count
    slot_iota = jnp.arange(capacity)
    hits = (expert_ids[:, :, None, None] == dest_expert[None, None, :, None]) & (
        expert_slots[:, :, None, None] == slot_iota[None, None, None, :]
    )
    hits_f = hits.astype(f32)
    dest_picks = jnp.sum(hits_f, 1).reshape(tokens_here, ep_count * capacity)
    dest_weights = jnp.sum(hits_f * route_gates[:, :, None, None], 1).reshape(
        tokens_here, ep_count * capacity
    )
    whole_rows = lax.all_gather(stream, "ep", axis=1, tiled=True).astype(f32)
    row_scale = lax.rsqrt(jnp.mean(whole_rows * whole_rows, -1, keepdims=True) + 1e-05)
    model_in = (whole_rows * row_scale * model_gain).astype(jnp.bfloat16)
    own_select = lax.dynamic_slice_in_dim(dest_picks, my_ep * capacity, capacity, 1).T.astype(
        jnp.bfloat16
    )
    expert_in = jnp.dot(own_select, model_in, preferred_element_type=f32).astype(jnp.bfloat16)
    w_gate = gate_weight[0]
    w_up = up_weight[0]
    w_down = down_weight[0]
    hidden_block = w_gate.shape[0]
    portion = lax.all_gather(expert_in, "ctx", axis=0, tiled=True)
    projected = jnp.concatenate([contract_last(portion, w_gate), contract_last(portion, w_up)], 1)
    pre_gate = projected[:, :hidden_block]
    pre_up = projected[:, hidden_block:]
    gate_sig = jax.nn.sigmoid(pre_gate)
    activated = (pre_gate * gate_sig * pre_up).astype(jnp.bfloat16)
    half_out = lax.psum_scatter(
        jnp.dot(activated, w_down, preferred_element_type=f32).astype(jnp.bfloat16),
        "ctx",
        scatter_dimension=0,
        tiled=True,
    )
    returned = lax.all_to_all(half_out, "ep", split_axis=1, concat_axis=0, tiled=True)
    expert_mix = jnp.dot(dest_weights, returned.astype(f32), precision=high)
    layer_out = (stream_f + expert_mix).astype(jnp.bfloat16)
    grad_out = out_grad.astype(f32)
    grad_send = jnp.dot(dest_weights.T, grad_out, precision=high).astype(jnp.bfloat16)
    grad_in = lax.all_to_all(grad_send, "ep", split_axis=0, concat_axis=1, tiled=True)
    grad_act = contract_last(lax.all_gather(grad_in, "ctx", axis=0, tiled=True), w_down)
    grad_gate_pre = (grad_act * pre_up * gate_sig * (1.0 + pre_gate * (1.0 - gate_sig))).astype(
        jnp.bfloat16
    )
    grad_up_pre = (grad_act * pre_gate * gate_sig).astype(jnp.bfloat16)
    grad_half = lax.psum_scatter(
        (
            jnp.dot(grad_gate_pre, w_gate, preferred_element_type=f32)
            + jnp.dot(grad_up_pre, w_up, preferred_element_type=f32)
        ).astype(jnp.bfloat16),
        "ctx",
        scatter_dimension=0,
        tiled=True,
    )
    grad_back = lax.all_to_all(grad_half, "ep", split_axis=1, concat_axis=0, tiled=True)
    grad_model_in = jnp.dot(dest_picks, grad_back.astype(f32), precision=high)
    scaled_grad = grad_model_in * gain_cols
    inner_sum = lax.psum(jnp.sum(stream_f * scaled_grad, -1), "ep")
    grad_stream = (
        grad_out
        + row_scale * scaled_grad
        - stream_f * row_scale**3 * inner_sum[:, None] / model_width
    ).astype(jnp.bfloat16)
    w_rows = lax.all_to_all(w_cols, "ep", split_axis=0, concat_axis=1, tiled=True)
    grad_heads = contract_last(lax.all_gather(grad_stream, "ep", axis=1, tiled=True), w_rows)
    head_pull = jax.vjp(lambda value: head_normalize(value, gain_heads), attended)[1]
    grad_attended = head_pull(grad_heads.reshape(tokens_here, head_count, head_size))[0].astype(
        jnp.bfloat16
    )
    state_part = jnp.einsum("thd,the->hde", query3, grad_attended, preferred_element_type=f32)
    later_sum = carried_in(state_part, "ctx", add_states, zero_state, True)
    state_total = lax.psum(state_part.astype(jnp.bfloat16), "ctx").astype(jnp.float32)
    grad_scores = jnp.einsum("the,she->hts", grad_attended, value3, preferred_element_type=f32)
    grad_masked = jnp.where(causal[None], grad_scores, 0.0).astype(jnp.bfloat16)
    grad_att_f = grad_attended.astype(f32)
    grad_query = jnp.einsum("the,hde->thd", grad_att_f, prefix, precision=high) + jnp.einsum(
        "hts,shd->thd", grad_masked, key3, preferred_element_type=f32
    )
    grad_key = jnp.einsum(
        "the,hde->thd", value3.astype(f32), later_sum, precision=high
    ) + jnp.einsum("hts,thd->shd", grad_masked, query3, preferred_element_type=f32)
    grad_value = jnp.einsum(
        "thd,hde->the", key3.astype(f32), later_sum, precision=high
    ) + jnp.einsum("hts,the->she", scores_bf, grad_attended, preferred_element_type=f32)
    flat_shape = (tokens_here, head_count * head_size)
    return (
        layer_out,
        grad_query.astype(jnp.bfloat16).reshape(flat_shape),
        grad_key.astype(jnp.bfloat16).reshape(flat_shape),
        grad_value.astype(jnp.bfloat16).reshape(flat_shape),
        state_total,
        grad_stream,
    )


def solution(mesh):
    return jax.shard_map(
        local,
        mesh=mesh,
        in_specs=(
            P("ctx", "ep"),
            P("ctx", "ep"),
            P("ctx", "ep"),
            P("ep", None, None),
            P("ep"),
            P("ctx", "ep"),
            P("ctx", "ep"),
            P(),
            P("ctx", None),
            P("ctx", None),
            P("ctx", None),
            P("ep", "ctx", None),
            P("ep", "ctx", None),
            P("ep", "ctx", None),
            P("ctx", "ep"),
        ),
        out_specs=(
            P("ctx", "ep"),
            P("ctx", "ep"),
            P("ctx", "ep"),
            P("ctx", "ep"),
            P("ep", None, None),
            P("ctx", "ep"),
        ),
        check_vma=False,
    )
```

profile of v0, /device:TPU:2, one launch (start us, length us, event | category | flops | bytes accessed | tf_op | source)
XLA Modules:
  0.0 797.9 jit_solution(11163868636489932232)
XLA Ops:
  12.9 72.9 %all-gather.15.cloned.1.call-done = bf16[32,128,128]{2,1,0:T(8,128)(2,1)} async-done(((bf16[2,128,128]{2,1,0:T(8,128)(2,1)}), bf16[32,128,128]{2,1,0:T(8,128)(2,1)}) %all-gather.15.cloned.1.call-update) | async-done | bytes 1048592 | tf_op jit(solution)/shard_map/all_gather | solution.py:11
  88.5 14.3 %all_to_all.67 = bf16[32,20,96]{2,1,0:T(8,128)(2,1)S(1)} all-to-all(bf16[32,20,96]{2,1,0:T(8,128)(2,1)S(1)} %all_to_all.53), channel_id=1, replica_groups=mesh['ctx'=16,'ep'=32] {'ep'}, dimensions={0} | all-to-all | bytes 245760 | tf_op jit(solution)/shard_map/all_to_all | solution.py:128
  104.0 52.8 %all-gather.13.cloned.1.call-done = bf16[8192,96]{0,1:T(8,128)(2,1)} async-done(((bf16[512,96]{0,1:T(8,128)(2,1)}), bf16[8192,96]{0,1:T(8,128)(2,1)}) %all-gather.13.cloned.1.call-update) | async-done | bytes 1572880 | tf_op jit(solution)/shard_map/all_gather | solution.py:83
  156.8 59.4 %all-gather.11.cloned.1.call-done = bf16[128,8192]{0,1:T(8,128)(2,1)} async-done(((bf16[128,256]{0,1:T(8,128)(2,1)}), bf16[128,8192]{0,1:T(8,128)(2,1)}) %all-gather.11.cloned.1.call-update) | async-done | bytes 2097168 | tf_op jit(solution)/shard_map/all_gather | solution.py:85
  216.3 2.6 fusion.33
  219.5 23.3 %all_gather.34 = bf16[128,3072]{0,1:T(8,128)(2,1)S(1)} all-gather(bf16[128,96]{0,1:T(8,128)(2,1)S(1)} %fusion.33), channel_id=1, replica_groups=mesh['ctx'=16,'ep'=32] {'ep'}, dimensions={1}, use_global_device_ids=true | all-gather | bytes 811008 | tf_op jit(solution)/shard_map/all_gather | solution.py:100
  246.5 6.2 all-to-all-start.3
  252.7 38.8 %all-gather.21.cloned.1.call-done = bf16[16,20,3072]{2,1,0:T(8,128)(2,1)} async-done(((bf16[1,20,3072]{2,1,0:T(8,128)(2,1)}), bf16[16,20,3072]{2,1,0:T(8,128)(2,1)}) %all-gather.21.cloned.1.call-update) | async-done | bytes 1966096 | tf_op jit(solution)/shard_map/all_gather | solution.py:129
  295.7 67.7 %all-gather.19.cloned.1.call-done = bf16[16,20,3072]{2,1,0:T(8,128)(2,1)} async-done(((bf16[1,20,3072]{2,1,0:T(8,128)(2,1)}), bf16[16,20,3072]{2,1,0:T(8,128)(2,1)}) %all-gather.19.cloned.1.call-update) | async-done | bytes 1966096 | tf_op jit(solution)/shard_map/all_gather | solution.py:111
  373.4 52.9 %fusion.70 = (bf16[24,3072]{1,0:T(8,128)(2,1)}, bf16[24,3072]{1,0:T(8,128)(2,1)}) fusion(bf16[320,3072]{1,0:T(8,128)(2,1)S(1)} %convolution_convert_fusion, bf16[320,3072]{1,0:T(8,128)(2,1)} %fusion.2), kind=kCustom, calls=%all-reduce-scatter.2 | all-reduce-scatter fusion | flops 2359297 | bytes 4229120
  427.3 5.2 collective-permute-start
  432.5 6.7 collective-permute-start.1
  440.9 4.2 collective-permute-start.3
  445.1 5.4 collective-permute-start.4
  451.5 5.0 collective-permute-start.5
  463.6 7.5 all-to-all-start.2
  474.1 4.1 all-to-all-done.2
  480.7 60.3 %psum.14 = f32[128]{0:T(128)S(1)} all-reduce(f32[128]{0:T(128)} %get-tuple-element.145), channel_id=1, replica_groups=mesh['ctx'=16,'ep'=32] {'ep'}, use_global_device_ids=true, to_apply=%region_9.10 | all-reduce | flops 128 | bytes 1024 | tf_op jit(solution)/shard_map/psum | solution.py:146
  542.5 27.4 %all_gather.37 = bf16[128,3072]{0,1:T(8,128)(2,1)S(1)} all-gather(bf16[128,96]{0,1:T(8,128)(2,1)S(1)} %fusion.59), channel_id=1, replica_groups=mesh['ctx'=16,'ep'=32] {'ep'}, dimensions={1}, use_global_device_ids=true | all-gather | bytes 811008 | tf_op jit(solution)/shard_map/all_gather | solution.py:153
  575.5 5.6 all-to-all-start
  582.5 5.7 all-to-all-done
  589.1 117.0 %all-reduce.7.cloned.1.call-done = bf16[2,128,128]{1,2,0:T(8,128)(2,1)} async-done(((bf16[2,128,128]{1,2,0:T(8,128)(2,1)}), bf16[2,128,128]{1,2,0:T(8,128)(2,1)}) %all-reduce.7.cloned.1.call-update) | async-done | bytes 65552 | tf_op jit(solution)/shard_map/psum | solution.py:160
  707.7 67.6 %all-gather.17.cloned.1.call-done = bf16[32,128,128]{2,1,0:T(8,128)(2,1)} async-done(((bf16[2,128,128]{2,1,0:T(8,128)(2,1)}), bf16[32,128,128]{2,1,0:T(8,128)(2,1)}) %all-gather.17.cloned.1.call-update) | async-done | bytes 1048592 | tf_op jit(solution)/shard_map/all_gather | solution.py:11
  775.3 13.4 %while.23 = (s32[]{:T(128)}, f32[2,128,128]{2,1,0:T(8,128)S(1)}, s32[]{:T(128)}, bf16[16,2,128,128]{3,2,1,0:T(8,128)(2,1)}, s32[]{:T(128)}, /*index=5*/s32[]{:T(128)}, s32[]{:T(128)}, s32[]{:T(128)}) while((s32[]{:T(128)}, f32[2,128,128]{2,1,0:T(8,128)S(1)}, s32[]{:T(128)}, bf16[16,2,128,128]{3,2,1,0:T(8,128)(2,1)}, s32[]{:T(128)}, ...), condition=%wide.region_12.13_spmd, body=%wide.region_11.12_spmd.sunk | while | flops 65542 | bytes 327815 | solution.py:18
  (182 shorter events, 69.3 us)
Async XLA Ops:
  7.2 286.8 %copy-start = (bf16[1,192,3072]{2,1,0:T(8,128)(2,1)S(1)}, bf16[1,192,3072]{2,1,0:T(8,128)(2,1)}, u32[]{:S(2)}) copy-start(bf16[1,192,3072]{2,1,0:T(8,128)(2,1)} %param.32) | copy-start | bytes 3538948
  7.2 78.7 %copy-start.24 = (f32[2,128,128]{2,1,0:T(8,128)S(1)}, f32[2,128,128]{2,1,0:T(8,128)}, u32[]{:S(2)}) copy-start(f32[2,128,128]{2,1,0:T(8,128)} %param.22) | copy-start | bytes 393220
  7.2 78.6 %all-gather.15.cloned.1.call-start = ((), (), s32[]{:S(2)}) async-start(), calls=%async_computation.7 | async-start | bytes 1114112 | tf_op jit(solution)/shard_map/all_gather | solution.py:11
  8.3 77.5 %copy-start.16 = (bf16[128,256]{0,1:T(8,128)(2,1)}, bf16[128,256]{0,1:T(8,128)(2,1)S(1)}, u32[]{:S(2)}) copy-start(bf16[128,256]{0,1:T(8,128)(2,1)S(1)} %copy.182) | copy-start | bytes 196612
  10.0 76.3 %copy-start.18 = (bf16[128,256]{1,0:T(8,128)(2,1)S(1)}, bf16[128,256]{1,0:T(8,128)(2,1)}, u32[]{:S(2)}) copy-start(bf16[128,256]{1,0:T(8,128)(2,1)} %param.21) | copy-start | bytes 196612
  10.0 146.8 %all-gather.13.cloned.1.call-start = ((), (), s32[]{:S(2)}) async-start(), calls=%async_computation.5 | async-start | bytes 1671168 | tf_op jit(solution)/shard_map/all_gather | solution.py:83
  10.7 205.5 %all-gather.11.cloned.1.call-start = ((), (), s32[]{:S(2)}) async-start(), calls=%async_computation.4 | async-start | bytes 2162688 | tf_op jit(solution)/shard_map/all_gather | solution.py:85
  87.3 204.1 %all-gather.21.cloned.1.call-start = ((), (), s32[]{:S(2)}) async-start(), calls=%async_computation.10 | async-start | bytes 2506752 | tf_op jit(solution)/shard_map/all_gather | solution.py:129
  87.9 128.3 %copy-start.27 = (bf16[128,96]{0,1:T(8,128)(2,1)S(1)}, bf16[128,96]{0,1:T(8,128)(2,1)}, u32[]{:S(2)}) copy-start(bf16[128,96]{0,1:T(8,128)(2,1)} %param.25) | copy-start | bytes 73732
  103.7 259.7 %all-gather.19.cloned.1.call-start = ((), (), s32[]{:S(2)}) async-start(), calls=%async_computation.9 | async-start | bytes 2506752 | tf_op jit(solution)/shard_map/all_gather | solution.py:111
  246.5 217.2 %all-to-all-start.3 = ((bf16[32,256,96]{1,2,0:T(8,128)(2,1)}), bf16[32,256,96]{1,2,0:T(8,128)(2,1)}, u32[]{:S(2)}, u32[]{:S(2)}) async-start(bf16[32,256,96]{1,2,0:T(8,128)(2,1)} %bitcast.161), calls=%async_computation.3 | async-start | bytes 3145728 | tf_op jit(solution)/shard_map/all_to_all | solution.py:152
  427.3 31.1 %collective-permute-start = (bf16[24,3072]{1,0:T(8,128)(2,1)}, bf16[24,3072]{1,0:T(8,128)(2,1)S(1)}, u32[]{:S(2)}, u32[]{:S(2)}) collective-permute-start(bf16[24,3072]{1,0:T(8,128)(2,1)} %get-tuple-element.139), channel_id=1, source_target_pairs={{0,32},{32,64},{64,96},{96,128},{128,160},{160,192},{192,224},{224... | collective-permute-start | bytes 442376
  432.5 25.9 %collective-permute-start.1 = (bf16[24,3072]{1,0:T(8,128)(2,1)}, bf16[24,3072]{1,0:T(8,128)(2,1)S(1)}, u32[]{:S(2)}, u32[]{:S(2)}) collective-permute-start(bf16[24,3072]{1,0:T(8,128)(2,1)} %get-tuple-element.139), channel_id=1, source_target_pairs={{0,64},{32,96},{64,128},{96,160},{128,192},{160,224},{192,256},{22... | collective-permute-start | bytes 442376
  439.3 12.2 %collective-permute-start.2 = (bf16[12,3072]{1,0:T(8,128)(2,1)S(1)}, bf16[12,3072]{1,0:T(8,128)(2,1)S(1)}, u32[]{:S(2)}, u32[]{:S(2)}) collective-permute-start(bf16[12,3072]{1,0:T(8,128)(2,1)S(1)} %slice), channel_id=1, source_target_pairs={{0,96},{32,128},{64,160},{96,192},{128,224},{160,256},{192,288},{2... | collective-permute-start | bytes 221192
  440.9 20.0 %collective-permute-start.3 = (bf16[24,3072]{1,0:T(8,128)(2,1)}, bf16[24,3072]{1,0:T(8,128)(2,1)S(1)}, u32[]{:S(2)}, u32[]{:S(2)}) collective-permute-start(bf16[24,3072]{1,0:T(8,128)(2,1)} %get-tuple-element.140), channel_id=1, source_target_pairs={{0,32},{32,64},{64,96},{96,128},{128,160},{160,192},{192,224},{224... | collective-permute-start | bytes 442376
  445.1 15.8 %collective-permute-start.4 = (bf16[24,3072]{1,0:T(8,128)(2,1)}, bf16[24,3072]{1,0:T(8,128)(2,1)S(1)}, u32[]{:S(2)}, u32[]{:S(2)}) collective-permute-start(bf16[24,3072]{1,0:T(8,128)(2,1)} %get-tuple-element.140), channel_id=1, source_target_pairs={{0,64},{32,96},{64,128},{96,160},{128,192},{160,224},{192,256},{22... | collective-permute-start | bytes 442376
  451.5 9.4 %collective-permute-start.5 = (bf16[12,3072]{1,0:T(8,128)(2,1)S(1)}, bf16[12,3072]{1,0:T(8,128)(2,1)S(1)}, u32[]{:S(2)}, u32[]{:S(2)}) collective-permute-start(bf16[12,3072]{1,0:T(8,128)(2,1)S(1)} %slice.1), channel_id=1, source_target_pairs={{0,96},{32,128},{64,160},{96,192},{128,224},{160,256},{192,288},{2... | collective-permute-start | bytes 221192
  463.6 14.6 %all-to-all-start.2 = ((bf16[20,32,96]{2,0,1:T(8,128)(2,1)}), bf16[20,32,96]{2,0,1:T(8,128)(2,1)}, u32[]{:S(2)}, u32[]{:S(2)}) async-start(bf16[20,32,96]{2,0,1:T(8,128)(2,1)} %copy.119), calls=%async_computation.2 | async-start | bytes 393216 | tf_op jit(solution)/shard_map/all_to_all | solution.py:143
  471.7 98.2 %copy-start.8 = (f32[128,2,128]{0,2,1:T(8,128)S(1)}, f32[128,2,128]{0,2,1:T(8,128)}, u32[]{:S(2)}) copy-start(f32[128,2,128]{0,2,1:T(8,128)} %copy-done.7) | copy-start | bytes 393220
  572.4 133.8 %all-reduce.7.cloned.1.call-start = ((), (), s32[]{:S(2)}) async-start(), calls=%async_computation.6 | async-start | bytes 131072 | tf_op jit(solution)/shard_map/psum | solution.py:160
  572.9 202.4 %all-gather.17.cloned.1.call-start = ((), (), s32[]{:S(2)}) async-start(), calls=%async_computation.8 | async-start | bytes 1114112 | tf_op jit(solution)/shard_map/all_gather | solution.py:11
  575.5 12.6 %all-to-all-start = ((bf16[20,32,96]{2,0,1:T(8,128)(2,1)}), bf16[20,32,96]{2,0,1:T(8,128)(2,1)S(1)}, u32[]{:S(2)}, u32[]{:S(2)}) async-start(bf16[20,32,96]{2,0,1:T(8,128)(2,1)} %copy.114), calls=%async_computation | async-start | bytes 393216 | tf_op jit(solution)/shard_map/all_to_all | solution.py:123
  581.6 207.1 %copy-start.21 = (bf16[128,256]{1,0:T(8,128)(2,1)S(1)}, bf16[128,256]{1,0:T(8,128)(2,1)}, u32[]{:S(2)}) copy-start(bf16[128,256]{1,0:T(8,128)(2,1)} %param.20) | copy-start | bytes 196612
  588.2 201.1 %copy-start.23 = (bf16[2,128,128]{2,1,0:T(8,128)(2,1)S(1)}, bf16[2,128,128]{2,1,0:T(8,128)(2,1)}, u32[]{:S(2)}) copy-start(bf16[2,128,128]{2,1,0:T(8,128)(2,1)} %copy-done.22) | copy-start | bytes 196612
  (30 other events, 401.8 us)
Sparse Core Ops, SparseCore 0:
  10.7 75.1 all-gather.14
  87.9 68.8 all-gather.12
  160.5 55.6 all-gather.10
  218.2 73.1 all-gather.20
  293.4 69.9 all-gather.18
  575.2 130.9 all-reduce.6
  708.8 66.4 all-gather.16
where the time goes:
time: 800 us; the launch traced here: 798 us
  waiting for transfers between devices  488 us (61%)
  blocking collectives  178 us (22%)
  starting transfers between devices  47.7 us (6%)
  local copies, waits for them, and re-layouts  29.8 us (4%)
  matrix products  22.5 us (3%)
  other arithmetic  15.8 us (2%)
  between operations  15.6 us (2%)
    all_gather x2, waiting for transfers between devices, carried_in(): gathered = lax.all_gather(value.astype(jnp.bfloat16), axis)  141 us
    psum x1, waiting for transfers between devices, local(): lax.psum(state_part.astype(jnp.bfloat16), 'ctx').astype(jnp.float32)  117 us
    all_gather x1, waiting for transfers between devices, local(): portion = lax.all_gather(expert_in, 'ctx', axis=0, tiled=True)  67.7 us
    psum x1, blocking collectives, local(): inner_sum = lax.psum(jnp.sum(stream_f * scaled_grad, -1), 'ep')  60.3 us
    all_gather x1, waiting for transfers between devices, local(): lax.all_gather(normed_heads, 'ep', axis=1, tiled=True)  59.4 us
    unnamed x1, blocking collectives  52.9 us
    all_gather x1, waiting for transfers between devices, local(): w_cols = lax.all_gather(out_weight, 'ctx', axis=0, tiled=True)  52.8 us
    all_gather x1, waiting for transfers between devices, local(): lax.all_gather(grad_in, 'ctx', axis=0, tiled=True)  38.8 us
  transfers between devices with their start and end apart: 16, of which 9 were waited for; matrix products, arithmetic and copies ran while one was open for 12% of the time, Pallas kernels for 0%

commit v1 on v0

--- a/solution.py
+++ b/solution.py
@@ -1,7 +1,40 @@
+import functools
 import jax
 import jax.numpy as jnp
 from jax import lax
 from jax.sharding import PartitionSpec as P
+from jax.lax import axis_index, axis_size, ppermute
+
+
+def pack_the_sections(matrix, chip_axis):
+    plain, long_array, block_next = (axis_size(chip_axis), axis_index(chip_axis), matrix.shape[0])
+    gallery = []
+    for ix, at in enumerate(matrix.shape):
+        gallery.append(at * plain if ix == 0 else at)
+    moved = local_next = matrix
+    upper = lax.dynamic_update_slice_in_dim(
+        jnp.zeros(gallery, matrix.dtype), matrix, long_array * block_next, axis=0
+    )
+    for k0 in range(1, plain // 2 + 1):
+        pieces_in = []
+        for ix in range(plain):
+            pieces_in.append((ix, (ix + 1) % plain))
+        moved = ppermute(moved, chip_axis, pieces_in)
+        upper = lax.dynamic_update_slice_in_dim(
+            upper, moved, (long_array - k0) % plain * block_next, axis=0
+        )
+        if 2 * k0 < plain:
+            xs_all = []
+            for ix in range(plain):
+                xs_all.append((ix, (ix - 1) % plain))
+            local_next = ppermute(local_next, chip_axis, xs_all)
+            upper = lax.dynamic_update_slice_in_dim(
+                upper, local_next, (long_array + k0) % plain * block_next, axis=0
+            )
+    return upper
+
+
+carry_the_routes_all = functools.partial(pack_the_sections, chip_axis="ctx")
 
 
 def carried_in(value, axis, join, neutral, backward):
@@ -80,7 +113,7 @@
         .astype(jnp.bfloat16)
         .reshape(tokens_here, head_count * head_size)
     )
-    w_cols = lax.all_gather(out_weight, "ctx", axis=0, tiled=True)
+    w_cols = carry_the_routes_all(out_weight)
     attn_proj = jnp.dot(
         lax.all_gather(normed_heads, "ep", axis=1, tiled=True), w_cols, preferred_element_type=f32
     )

time: 800 us -> 737 us (0.921)
  waiting for transfers between devices: 488 us -> 360 us
  starting transfers between devices: 47.7 us -> 112 us
    ppermute x0 -> x15, starting transfers between devices: none -> 64.3 us  [the longest x7 46.5 us: pack_the_sections(): local_next = ppermute(local_next, chip_axis, xs_all)]
    all_gather x1, waiting for transfers between devices: 59.4 us -> 0.02 us  [local(): lax.all_gather(normed_heads, 'ep', axis=1, tiled=True)]
    all_gather x1 -> x0, waiting for transfers between devices: 52.8 us -> none  [local(): w_cols = lax.all_gather(out_weight, 'ctx', axis=0, tiled=True)]
    all_gather x1, waiting for transfers between devices: 38.8 us -> 11.2 us  [local(): lax.all_gather(grad_in, 'ctx', axis=0, tiled=True)]
    ppermute x0 -> x15, waiting for transfers between devices: none -> 12.2 us  [the longest x8 12.2 us: pack_the_sections(): moved = ppermute(moved, chip_axis, pieces_in)]
    unnamed x89 -> x87, local copies, waits for them, and re-layouts: 19.3 us -> 19.3 us
  transfers between devices with their start and end apart: 16 -> 30, of which waited for: 9 -> 15; matrix products, arithmetic and copies ran while one was open for 12% -> 13% of each run, Pallas kernels for 0% -> 0%
where the time goes in v1:
time: 737 us; the launch traced here: 735 us
  waiting for transfers between devices  360 us (49%)
  blocking collectives  178 us (24%)
  starting transfers between devices  112 us (15%)
  local copies, waits for them, and re-layouts  30.4 us (4%)
  matrix products  22 us (3%)
  between operations  16.2 us (2%)
  other arithmetic  15.8 us (2%)
    all_gather x2, waiting for transfers between devices, carried_in(): gathered = lax.all_gather(value.astype(jnp.bfloat16), axis)  141 us
    psum x1, waiting for transfers between devices, local(): lax.psum(state_part.astype(jnp.bfloat16), 'ctx').astype(jnp.float32)  117 us
    all_gather x1, waiting for transfers between devices, local(): portion = lax.all_gather(expert_in, 'ctx', axis=0, tiled=True)  67.6 us
    psum x1, blocking collectives, local(): inner_sum = lax.psum(jnp.sum(stream_f * scaled_grad, -1), 'ep')  60.3 us
    unnamed x1, blocking collectives  52.9 us
    ppermute x7, starting transfers between devices, pack_the_sections(): local_next = ppermute(local_next, chip_axis, xs_all)  46.5 us
    unnamed x6, starting transfers between devices  28.1 us
    all_gather x1, blocking collectives, local(): lax.all_gather(grad_stream, 'ep', axis=1, tiled=True)  27.4 us
  transfers between devices with their start and end apart: 30, of which 15 were waited for; matrix products, arithmetic and copies ran while one was open for 13% of the time, Pallas kernels for 0%

profile of v1, /device:TPU:2, one launch (start us, length us, event | category | flops | bytes accessed | tf_op | source)
XLA Modules:
  0.0 734.5 jit_solution(17222544006566006718)
XLA Ops:
  12.1 73.7 %all-gather.12.cloned.1.call-done = bf16[32,128,128]{2,1,0:T(8,128)(2,1)} async-done(((bf16[2,128,128]{2,1,0:T(8,128)(2,1)}), bf16[32,128,128]{2,1,0:T(8,128)(2,1)}) %all-gather.12.cloned.1.call-update) | async-done | bytes 1048592 | tf_op jit(solution)/shard_map/all_gather | solution.py:44
  88.5 14.3 %all_to_all.67 = bf16[32,20,96]{2,1,0:T(8,128)(2,1)S(1)} all-to-all(bf16[32,20,96]{2,1,0:T(8,128)(2,1)S(1)} %all_to_all.53), channel_id=1, replica_groups=mesh['ctx'=16,'ep'=32] {'ep'}, dimensions={0} | all-to-all | bytes 245760 | tf_op jit(solution)/shard_map/all_to_all | solution.py:161
  108.2 15.6 %collective-permute-start.1 = (bf16[512,96]{0,1:T(8,128)(2,1)S(1)}, bf16[512,96]{0,1:T(8,128)(2,1)S(1)}, u32[]{:S(2)}, u32[]{:S(2)}) collective-permute-start(bf16[512,96]{0,1:T(8,128)(2,1)S(1)} %copy-done.25), channel_id=1, source_target_pairs={{0,480},{32,0},{64,32},{96,64},{128,96},{160,128},{192,160},{224,1... | collective-permute-start | bytes 294920 | tf_op jit(solution)/shard_map/ppermute | solution.py:30
  127.1 5.1 collective-permute-start.3
  134.8 5.1 collective-permute-start.5
  142.5 5.1 collective-permute-start.7
  165.7 5.2 collective-permute-start.13
  174.4 7.1 collective-permute-done.14
  184.3 22.8 %all_gather.30 = bf16[128,3072]{0,1:T(8,128)(2,1)S(1)} all-gather(bf16[128,96]{0,1:T(8,128)(2,1)S(1)} %fusion.33), channel_id=1, replica_groups=mesh['ctx'=16,'ep'=32] {'ep'}, dimensions={1}, use_global_device_ids=true | all-gather | bytes 811008 | tf_op jit(solution)/shard_map/all_gather | solution.py:133
  210.8 6.0 all-to-all-start.3
  216.8 11.2 %all-gather.18.cloned.1.call-done = bf16[16,20,3072]{2,1,0:T(8,128)(2,1)} async-done(((bf16[1,20,3072]{2,1,0:T(8,128)(2,1)}), bf16[16,20,3072]{2,1,0:T(8,128)(2,1)}) %all-gather.18.cloned.1.call-update) | async-done | bytes 1966096 | tf_op jit(solution)/shard_map/all_gather | solution.py:162
  232.3 67.6 %all-gather.16.cloned.1.call-done = bf16[16,20,3072]{2,1,0:T(8,128)(2,1)} async-done(((bf16[1,20,3072]{2,1,0:T(8,128)(2,1)}), bf16[16,20,3072]{2,1,0:T(8,128)(2,1)}) %all-gather.16.cloned.1.call-update) | async-done | bytes 1966096 | tf_op jit(solution)/shard_map/all_gather | solution.py:144
  310.0 52.9 %fusion.70 = (bf16[24,3072]{1,0:T(8,128)(2,1)}, bf16[24,3072]{1,0:T(8,128)(2,1)}) fusion(bf16[320,3072]{1,0:T(8,128)(2,1)S(1)} %convolution_convert_fusion, bf16[320,3072]{1,0:T(8,128)(2,1)} %fusion.2), kind=kCustom, calls=%all-reduce-scatter.2 | all-reduce-scatter fusion | flops 2359297 | bytes 4229120
  363.9 5.3 collective-permute-start.15
  369.1 6.7 collective-permute-start.16
  381.7 5.4 collective-permute-start.19
  400.1 7.5 %all-to-all-start.2 = ((bf16[20,32,96]{2,0,1:T(8,128)(2,1)}), bf16[20,32,96]{2,0,1:T(8,128)(2,1)}, u32[]{:S(2)}, u32[]{:S(2)}) async-start(bf16[20,32,96]{2,0,1:T(8,128)(2,1)} %copy.118), calls=%async_computation.2 | async-start | bytes 393216 | tf_op jit(solution)/shard_map/all_to_all | solution.py:176
  417.2 60.3 %psum.14 = f32[128]{0:T(128)S(1)} all-reduce(f32[128]{0:T(128)} %get-tuple-element.145), channel_id=1, replica_groups=mesh['ctx'=16,'ep'=32] {'ep'}, use_global_device_ids=true, to_apply=%region_9.10 | all-reduce | flops 128 | bytes 1024 | tf_op jit(solution)/shard_map/psum | solution.py:179
  478.9 27.4 %all_gather.33 = bf16[128,3072]{0,1:T(8,128)(2,1)S(1)} all-gather(bf16[128,96]{0,1:T(8,128)(2,1)S(1)} %fusion.59), channel_id=1, replica_groups=mesh['ctx'=16,'ep'=32] {'ep'}, dimensions={1}, use_global_device_ids=true | all-gather | bytes 811008 | tf_op jit(solution)/shard_map/all_gather | solution.py:186
  511.9 5.6 all-to-all-start
  518.8 5.7 all-to-all-done
  525.5 117.4 %all-reduce.7.cloned.1.call-done = bf16[2,128,128]{1,2,0:T(8,128)(2,1)} async-done(((bf16[2,128,128]{1,2,0:T(8,128)(2,1)}), bf16[2,128,128]{1,2,0:T(8,128)(2,1)}) %all-reduce.7.cloned.1.call-update) | async-done | bytes 65552 | tf_op jit(solution)/shard_map/psum | solution.py:193
  644.5 67.4 %all-gather.14.cloned.1.call-done = bf16[32,128,128]{2,1,0:T(8,128)(2,1)} async-done(((bf16[2,128,128]{2,1,0:T(8,128)(2,1)}), bf16[32,128,128]{2,1,0:T(8,128)(2,1)}) %all-gather.14.cloned.1.call-update) | async-done | bytes 1048592 | tf_op jit(solution)/shard_map/all_gather | solution.py:44
  711.9 13.4 %while.23 = (s32[]{:T(128)}, f32[2,128,128]{2,1,0:T(8,128)S(1)}, s32[]{:T(128)}, bf16[16,2,128,128]{3,2,1,0:T(8,128)(2,1)}, s32[]{:T(128)}, /*index=5*/s32[]{:T(128)}, s32[]{:T(128)}, s32[]{:T(128)}) while((s32[]{:T(128)}, f32[2,128,128]{2,1,0:T(8,128)S(1)}, s32[]{:T(128)}, bf16[16,2,128,128]{3,2,1,0:T(8,128)(2,1)}, s32[]{:T(128)}, ...), condition=%wide.region_12.13_spmd, body=%wide.region_11.12_spmd.sunk | while | flops 65542 | bytes 327815 | solution.py:51
  (224 shorter events, 117.4 us)
Async XLA Ops:
  7.2 78.6 %all-gather.12.cloned.1.call-start = ((), (), s32[]{:S(2)}) async-start(), calls=%async_computation.6 | async-start | bytes 1114112 | tf_op jit(solution)/shard_map/all_gather | solution.py:44
  10.0 171.6 %all-gather.10.cloned.1.call-start = ((), (), s32[]{:S(2)}) async-start(), calls=%async_computation.4 | async-start | bytes 2162688 | tf_op jit(solution)/shard_map/all_gather | solution.py:118
  87.3 140.7 %all-gather.18.cloned.1.call-start = ((), (), s32[]{:S(2)}) async-start(), calls=%async_computation.9 | async-start | bytes 2506752 | tf_op jit(solution)/shard_map/all_gather | solution.py:162
  103.7 196.2 %all-gather.16.cloned.1.call-start = ((), (), s32[]{:S(2)}) async-start(), calls=%async_computation.8 | async-start | bytes 2506752 | tf_op jit(solution)/shard_map/all_gather | solution.py:144
  103.8 21.4 %collective-permute-start = (bf16[512,96]{0,1:T(8,128)(2,1)S(1)}, bf16[512,96]{0,1:T(8,128)(2,1)S(1)}, u32[]{:S(2)}, u32[]{:S(2)}) collective-permute-start(bf16[512,96]{0,1:T(8,128)(2,1)S(1)} %copy-done.25), channel_id=1, source_target_pairs={{0,32},{32,64},{64,96},{96,128},{128,160},{160,192},{192,224},{224... | collective-permute-start | bytes 294920 | tf_op jit(solution)/shard_map/ppermute | solution.py:22
  108.2 18.9 %collective-permute-start.1 = (bf16[512,96]{0,1:T(8,128)(2,1)S(1)}, bf16[512,96]{0,1:T(8,128)(2,1)S(1)}, u32[]{:S(2)}, u32[]{:S(2)}) collective-permute-start(bf16[512,96]{0,1:T(8,128)(2,1)S(1)} %copy-done.25), channel_id=1, source_target_pairs={{0,480},{32,0},{64,32},{96,64},{128,96},{160,128},{192,160},{224,1... | collective-permute-start | bytes 294920 | tf_op jit(solution)/shard_map/ppermute | solution.py:30
  125.2 7.7 %collective-permute-start.2 = (bf16[512,96]{0,1:T(8,128)(2,1)S(1)}, bf16[512,96]{0,1:T(8,128)(2,1)S(1)}, u32[]{:S(2)}, u32[]{:S(2)}) collective-permute-start(bf16[512,96]{0,1:T(8,128)(2,1)S(1)} %collective-permute-done), channel_id=1, source_target_pairs={{0,32},{32,64},{64,96},{96,128},{128,160},{160,192},{192,224},{224... | collective-permute-start | bytes 294920 | tf_op jit(solution)/shard_map/ppermute | solution.py:22
  132.9 7.7 %collective-permute-start.4 = (bf16[512,96]{0,1:T(8,128)(2,1)S(1)}, bf16[512,96]{0,1:T(8,128)(2,1)S(1)}, u32[]{:S(2)}, u32[]{:S(2)}) collective-permute-start(bf16[512,96]{0,1:T(8,128)(2,1)S(1)} %collective-permute-done.2), channel_id=1, source_target_pairs={{0,32},{32,64},{64,96},{96,128},{128,160},{160,192},{192,224},{224... | collective-permute-start | bytes 294920 | tf_op jit(solution)/shard_map/ppermute | solution.py:22
  140.6 7.7 %collective-permute-start.6 = (bf16[512,96]{0,1:T(8,128)(2,1)S(1)}, bf16[512,96]{0,1:T(8,128)(2,1)S(1)}, u32[]{:S(2)}, u32[]{:S(2)}) collective-permute-start(bf16[512,96]{0,1:T(8,128)(2,1)S(1)} %collective-permute-done.4), channel_id=1, source_target_pairs={{0,32},{32,64},{64,96},{96,128},{128,160},{160,192},{192,224},{224... | collective-permute-start | bytes 294920 | tf_op jit(solution)/shard_map/ppermute | solution.py:22
  148.3 7.7 %collective-permute-start.8 = (bf16[512,96]{0,1:T(8,128)(2,1)S(1)}, bf16[512,96]{0,1:T(8,128)(2,1)S(1)}, u32[]{:S(2)}, u32[]{:S(2)}) collective-permute-start(bf16[512,96]{0,1:T(8,128)(2,1)S(1)} %collective-permute-done.6), channel_id=1, source_target_pairs={{0,32},{32,64},{64,96},{96,128},{128,160},{160,192},{192,224},{224... | collective-permute-start | bytes 294920 | tf_op jit(solution)/shard_map/ppermute | solution.py:22
  163.7 8.7 %collective-permute-start.12 = (bf16[512,96]{0,1:T(8,128)(2,1)S(1)}, bf16[512,96]{0,1:T(8,128)(2,1)S(1)}, u32[]{:S(2)}, u32[]{:S(2)}) collective-permute-start(bf16[512,96]{0,1:T(8,128)(2,1)S(1)} %collective-permute-done.10), channel_id=1, source_target_pairs={{0,32},{32,64},{64,96},{96,128},{128,160},{160,192},{192,224},{224... | collective-permute-start | bytes 294920 | tf_op jit(solution)/shard_map/ppermute | solution.py:22
  165.7 8.7 %collective-permute-start.13 = (bf16[512,96]{0,1:T(8,128)(2,1)S(1)}, bf16[512,96]{0,1:T(8,128)(2,1)S(1)}, u32[]{:S(2)}, u32[]{:S(2)}) collective-permute-start(bf16[512,96]{0,1:T(8,128)(2,1)S(1)} %collective-permute-done.11), channel_id=1, source_target_pairs={{0,480},{32,0},{64,32},{96,64},{128,96},{160,128},{192,160},{224,1... | collective-permute-start | bytes 294920 | tf_op jit(solution)/shard_map/ppermute | solution.py:30
  172.4 9.1 %collective-permute-start.14 = (bf16[512,96]{0,1:T(8,128)(2,1)S(1)}, bf16[512,96]{0,1:T(8,128)(2,1)S(1)}, u32[]{:S(2)}, u32[]{:S(2)}) collective-permute-start(bf16[512,96]{0,1:T(8,128)(2,1)S(1)} %collective-permute-done.12), channel_id=1, source_target_pairs={{0,32},{32,64},{64,96},{96,128},{128,160},{160,192},{192,224},{224... | collective-permute-start | bytes 294920 | tf_op jit(solution)/shard_map/ppermute | solution.py:22
  210.8 189.3 %all-to-all-start.3 = ((bf16[32,256,96]{1,2,0:T(8,128)(2,1)}), bf16[32,256,96]{1,2,0:T(8,128)(2,1)}, u32[]{:S(2)}, u32[]{:S(2)}) async-start(bf16[32,256,96]{1,2,0:T(8,128)(2,1)} %bitcast.161), calls=%async_computation.3 | async-start | bytes 3145728 | tf_op jit(solution)/shard_map/all_to_all | solution.py:185
  363.9 31.0 %collective-permute-start.15 = (bf16[24,3072]{1,0:T(8,128)(2,1)}, bf16[24,3072]{1,0:T(8,128)(2,1)S(1)}, u32[]{:S(2)}, u32[]{:S(2)}) collective-permute-start(bf16[24,3072]{1,0:T(8,128)(2,1)} %get-tuple-element.139), channel_id=1, source_target_pairs={{0,32},{32,64},{64,96},{96,128},{128,160},{160,192},{192,224},{224... | collective-permute-start | bytes 442376
  369.1 25.7 %collective-permute-start.16 = (bf16[24,3072]{1,0:T(8,128)(2,1)}, bf16[24,3072]{1,0:T(8,128)(2,1)S(1)}, u32[]{:S(2)}, u32[]{:S(2)}) collective-permute-start(bf16[24,3072]{1,0:T(8,128)(2,1)} %get-tuple-element.139), channel_id=1, source_target_pairs={{0,64},{32,96},{64,128},{96,160},{128,192},{160,224},{192,256},{22... | collective-permute-start | bytes 442376
  375.9 12.2 %collective-permute-start.17 = (bf16[12,3072]{1,0:T(8,128)(2,1)S(1)}, bf16[12,3072]{1,0:T(8,128)(2,1)S(1)}, u32[]{:S(2)}, u32[]{:S(2)}) collective-permute-start(bf16[12,3072]{1,0:T(8,128)(2,1)S(1)} %slice), channel_id=1, source_target_pairs={{0,96},{32,128},{64,160},{96,192},{128,224},{160,256},{192,288},{2... | collective-permute-start | bytes 221192
  377.5 19.8 %collective-permute-start.18 = (bf16[24,3072]{1,0:T(8,128)(2,1)}, bf16[24,3072]{1,0:T(8,128)(2,1)S(1)}, u32[]{:S(2)}, u32[]{:S(2)}) collective-permute-start(bf16[24,3072]{1,0:T(8,128)(2,1)} %get-tuple-element.140), channel_id=1, source_target_pairs={{0,32},{32,64},{64,96},{96,128},{128,160},{160,192},{192,224},{224... | collective-permute-start | bytes 442376
  381.7 15.6 %collective-permute-start.19 = (bf16[24,3072]{1,0:T(8,128)(2,1)}, bf16[24,3072]{1,0:T(8,128)(2,1)S(1)}, u32[]{:S(2)}, u32[]{:S(2)}) collective-permute-start(bf16[24,3072]{1,0:T(8,128)(2,1)} %get-tuple-element.140), channel_id=1, source_target_pairs={{0,64},{32,96},{64,128},{96,160},{128,192},{160,224},{192,256},{22... | collective-permute-start | bytes 442376
  388.1 9.3 %collective-permute-start.20 = (bf16[12,3072]{1,0:T(8,128)(2,1)S(1)}, bf16[12,3072]{1,0:T(8,128)(2,1)S(1)}, u32[]{:S(2)}, u32[]{:S(2)}) collective-permute-start(bf16[12,3072]{1,0:T(8,128)(2,1)S(1)} %slice.1), channel_id=1, source_target_pairs={{0,96},{32,128},{64,160},{96,192},{128,224},{160,256},{192,288},{2... | collective-permute-start | bytes 221192
  400.1 14.6 %all-to-all-start.2 = ((bf16[20,32,96]{2,0,1:T(8,128)(2,1)}), bf16[20,32,96]{2,0,1:T(8,128)(2,1)}, u32[]{:S(2)}, u32[]{:S(2)}) async-start(bf16[20,32,96]{2,0,1:T(8,128)(2,1)} %copy.118), calls=%async_computation.2 | async-start | bytes 393216 | tf_op jit(solution)/shard_map/all_to_all | solution.py:176
  508.8 134.0 %all-reduce.7.cloned.1.call-start = ((), (), s32[]{:S(2)}) async-start(), calls=%async_computation.5 | async-start | bytes 131072 | tf_op jit(solution)/shard_map/psum | solution.py:193
  509.4 202.5 %all-gather.14.cloned.1.call-start = ((), (), s32[]{:S(2)}) async-start(), calls=%async_computation.7 | async-start | bytes 1114112 | tf_op jit(solution)/shard_map/all_gather | solution.py:44
  511.9 12.6 %all-to-all-start = ((bf16[20,32,96]{2,0,1:T(8,128)(2,1)}), bf16[20,32,96]{2,0,1:T(8,128)(2,1)S(1)}, u32[]{:S(2)}, u32[]{:S(2)}) async-start(bf16[20,32,96]{2,0,1:T(8,128)(2,1)} %copy.113), calls=%async_computation | async-start | bytes 393216 | tf_op jit(solution)/shard_map/all_to_all | solution.py:156
  (43 other events, 1422.4 us)
Sparse Core Ops, SparseCore 0:
  10.7 75.1 all-gather.11
  89.5 63.0 all-gather.9
  154.7 73.2 all-gather.17
  230.0 69.8 all-gather.15
  511.7 131.1 all-reduce.6
  645.4 66.4 all-gather.13
